TPU v7x, 512 devices: a whole 4x4x16 slice. The times are simulated.
512 devices in a mesh: tok: 64 (over z, x), head: 8 (over y, core).
Axes of the slice: x: 4, y: 4, z: 16, core: 2. Of those that a mesh axis runs over, the one named last changes fastest.
Arguments:
- tokens: bfloat16 [32768, 2560], P('tok', 'head'), may hold values from -6 to 6
- query_weight: bfloat16 [2560, 2560], P('tok'), may hold values from -0.125 to 0.125
- keyvalue_weight: bfloat16 [2560, 512], P('tok'), may hold values from -0.125 to 0.125
- output_weight: bfloat16 [2560, 2560], P(None, ('head', 'tok')), may hold values from -0.125 to 0.125
- cache: bfloat16 [2048, 2, 128, 256], P(('tok', 'head')), may hold values from -460 to 460
- page_table: int32 [512, 4], P('tok'), may hold values from 0 to 2047, as said below
- parents: int32 [512, 64], P('tok'), may hold values from 0 to 62, as said below
- cache_len: int32 [512], P('tok'), may hold values from 1 to 448, as said below
- accepted_leaf: int32 [512], P('tok'), may hold values from 0 to 63
Outputs:
- attended: bfloat16 [32768, 2560], P('tok', 'head')
- cache_out: bfloat16 [2048, 2, 128, 256], P(('tok', 'head'))
Inputs may be any that keep to these rules, and one draw needn't show every extreme that they name: `page_table`: for every d, row d names each of the pages d * 4 to d * 4 + 3 exactly once, so request d's pages all lie on device d (devices counted tok-major, head-minor). parents[r, 0] = 0, and parents[r, i] < i for i >= 1. `cache_len`: roughly half of the requests hold at most 128 cached positions, the others more than 320.
All inputs are finite; a program needn't handle non-finite values.
Results may differ from a plain program's by a relative error of at most 0.014.
The roundings to bfloat16 on the way count: a program that leaves them out, or rounds other values in their place, can miss the bound.
Values may be sent and summed in bfloat16 or wider, within the bound.
No kernel may reach another device: no remote copies, remote signals or barrier semaphores. Data moves between devices by JAX's collectives and lax.ppermute only.
A program may use at most 64 MiB of HBM per device.

v0:
```python
import math
import jax
import jax.numpy as jnp
from jax import lax
from jax.sharding import PartitionSpec as P

HQ = 10
HD = 256
DRAFT = 64
PAGE = 128
NPR = 4
WINDOW = 256


def ancestry(parent_row):
    node_ids = jnp.arange(DRAFT, dtype=jnp.int32)
    link = (parent_row[:, None] == node_ids[None, :]).astype(jnp.float32)
    reach = jnp.minimum(link + jnp.eye(DRAFT, dtype=jnp.float32), 1.0)
    for sweep in range((DRAFT - 1).bit_length()):
        reach = jnp.minimum(jnp.dot(reach, reach, precision=lax.Precision.HIGHEST), 1.0)
    depth = (jnp.sum(reach, axis=1) - 1.0).astype(jnp.int32)
    return (reach, depth)


def rotate(values, position):
    half = HD // 4
    freq = jnp.exp(jnp.arange(half, dtype=jnp.float32) * (-2.0 * math.log(10000.0) / (HD // 2)))
    angle = position.astype(jnp.float32)[..., None] * freq
    cosine = jnp.cos(angle)
    sine = jnp.sin(angle)
    first = values[..., :half]
    second = values[..., half : 2 * half]
    return jnp.concatenate(
        [first * cosine - second * sine, second * cosine + first * sine, values[..., 2 * half :]],
        axis=-1,
    )


def attend(queries, cache_keys, cache_values, tree_keys, tree_values, lengths, position, reach):
    window_span = cache_keys.shape[1]
    slot_ids = jnp.arange(window_span, dtype=jnp.int32)
    visible = (slot_ids[None, None, :] < lengths[:, None, None]) & (
        slot_ids[None, None, :] > position[:, :, None] - WINDOW
    )
    cache_scores = jnp.einsum(
        "rnhd,rcd->rhnc", queries, cache_keys, preferred_element_type=jnp.float32
    )
    tree_scores = jnp.einsum(
        "rnhd,rmd->rhnm", queries, tree_keys, preferred_element_type=jnp.float32
    )
    cache_scores = jnp.where(visible[:, None], cache_scores, -1e30)
    tree_scores = jnp.where(reach[:, None] > 0.5, tree_scores, -1e30)
    row_peak = jnp.maximum(jnp.max(cache_scores, axis=-1), jnp.max(tree_scores, axis=-1))[..., None]
    cache_weights = jnp.exp(cache_scores - row_peak)
    tree_weights = jnp.exp(tree_scores - row_peak)
    denominator = jnp.sum(cache_weights, axis=-1, keepdims=True) + jnp.sum(
        tree_weights, axis=-1, keepdims=True
    )
    cache_weights = (cache_weights / denominator).astype(jnp.bfloat16)
    tree_weights = (tree_weights / denominator).astype(jnp.bfloat16)
    result = jnp.einsum(
        "rhnc,rcd->rnhd", cache_weights, cache_values, preferred_element_type=jnp.float32
    )
    result = result + jnp.einsum(
        "rhnm,rmd->rnhd", tree_weights, tree_values, preferred_element_type=jnp.float32
    )
    return result.astype(jnp.bfloat16)


def refresh(logical_pages, length, leaf, reach, depth, new_keys, new_values):
    count = logical_pages.shape[0] * logical_pages.shape[2]
    logical = jnp.transpose(logical_pages, (1, 0, 2, 3)).reshape(2, count, HD)
    slot_ids = jnp.arange(count, dtype=jnp.int32)
    on_path = reach[leaf]
    selector = ((on_path[None, :] > 0.5) & (depth[None, :] == slot_ids[:, None] - length)).astype(
        jnp.float32
    )
    placed_keys = jnp.dot(selector, new_keys.astype(jnp.float32), precision=lax.Precision.HIGHEST)
    placed_values = jnp.dot(
        selector, new_values.astype(jnp.float32), precision=lax.Precision.HIGHEST
    )
    placed = jnp.stack([placed_keys, placed_values]).astype(jnp.bfloat16)
    written = jnp.sum(selector, axis=1) > 0.5
    logical = jnp.where(written[None, :, None], placed, logical)
    return jnp.transpose(
        logical.reshape(2, logical_pages.shape[0], logical_pages.shape[2], HD), (1, 0, 2, 3)
    )


def contract(source, piece):
    return jnp.dot(source, piece, preferred_element_type=jnp.float32)


def project_memory(rows, keyvalue_weight, position):
    projected = contract(rows, lax.all_gather(keyvalue_weight, "tok", axis=0, tiled=True))
    new_keys = rotate(projected[:, :HD], position).astype(jnp.bfloat16)
    new_values = projected[:, HD:].astype(jnp.bfloat16)
    return (new_keys, new_values)


def split_pages(page_blocks, count):
    cache_keys = page_blocks[:, :, 0].reshape(count, NPR * PAGE, HD)
    cache_values = page_blocks[:, :, 1].reshape(count, NPR * PAGE, HD)
    return (cache_keys, cache_values)


def reduce_heads(mixed, output_weight, safe_heads, head_mask, slots_per):
    head_count = lax.axis_size("head")
    tok_count = lax.axis_size("tok")
    narrow = output_weight.shape[1]
    blocks = lax.all_gather(output_weight, "head", axis=1, tiled=True)
    part_cols = blocks.shape[1]
    my_output_weight = (
        jnp.take(blocks.reshape(HQ, HD, part_cols), safe_heads, axis=0) * head_mask[:, None, None]
    )
    my_output_weight = my_output_weight.reshape(slots_per * HD, part_cols)
    partial_value = jnp.dot(
        mixed,
        lax.all_gather(my_output_weight, "tok", axis=1, tiled=True),
        preferred_element_type=jnp.float32,
    ).astype(jnp.bfloat16)
    row_count = partial_value.shape[0]
    partial_value = partial_value.reshape(row_count, tok_count, head_count, narrow)
    partial_value = jnp.transpose(partial_value, (0, 2, 1, 3)).reshape(
        row_count, tok_count * head_count * narrow
    )
    partial_value = lax.optimization_barrier(partial_value)
    summed = lax.psum_scatter(
        partial_value.astype(jnp.float32).astype(jnp.bfloat16),
        "head",
        scatter_dimension=1,
        tiled=True,
    )
    return summed


def shards(
    tokens,
    query_weight,
    keyvalue_weight,
    output_weight,
    cache,
    page_table,
    parents,
    cache_len,
    accepted_leaf,
):
    head_count = lax.axis_size("head")
    head_index = lax.axis_index("head")
    tok_index = lax.axis_index("tok")
    slots_per = -(-HQ // head_count)
    requests = parents.shape[0]
    owned = requests // head_count
    rows_owned = owned * DRAFT
    pages_dev = cache.shape[0]
    gathered = lax.all_gather(tokens, "head", axis=1, tiled=True)
    wide = gathered.astype(jnp.float32)
    mean_square = jnp.mean(wide * wide, axis=1, keepdims=True)
    normed = (wide * lax.rsqrt(mean_square + 1e-06)).astype(jnp.bfloat16)
    reach, depth = jax.vmap(ancestry)(parents)
    position = cache_len[:, None] + depth
    flat_pos = position.reshape(-1)
    head_ids = head_index + head_count * jnp.arange(slots_per, dtype=jnp.int32)
    usable = head_ids < HQ
    safe_heads = jnp.minimum(head_ids, HQ - 1)
    head_mask = usable.astype(jnp.bfloat16)
    part_rows = query_weight.shape[0]
    my_query_weight = (
        jnp.take(query_weight.reshape(part_rows, HQ, HD), safe_heads, axis=1)
        * head_mask[None, :, None]
    )
    my_query_weight = my_query_weight.reshape(part_rows, slots_per * HD)
    queries = contract(normed, lax.all_gather(my_query_weight, "tok", axis=0, tiled=True))
    queries = (rotate(queries.reshape(-1, slots_per, HD), flat_pos[:, None]) * HD ** (-0.5)).astype(
        jnp.bfloat16
    )
    own_start = head_index * rows_owned
    own_reach = lax.dynamic_slice_in_dim(reach, head_index * owned, owned, 0)
    own_depth = lax.dynamic_slice_in_dim(depth, head_index * owned, owned, 0)
    own_len = lax.dynamic_slice_in_dim(cache_len, head_index * owned, owned, 0)
    own_leaf = lax.dynamic_slice_in_dim(accepted_leaf, head_index * owned, owned, 0)
    device = tok_index * head_count + head_index
    own_table = (
        lax.dynamic_slice_in_dim(page_table, head_index * owned, owned, 0) - device * pages_dev
    )
    own_pages = jnp.take(cache, own_table.reshape(-1), axis=0).reshape(owned, NPR, 2, PAGE, HD)
    tree_keys, tree_values = project_memory(normed, keyvalue_weight, flat_pos)
    own_keys = lax.dynamic_slice_in_dim(tree_keys, own_start, rows_owned, 0)
    own_values = lax.dynamic_slice_in_dim(tree_values, own_start, rows_owned, 0)
    page_pool = lax.all_gather(cache, "head", axis=0, tiled=True)
    local_ids = page_table - tok_index * head_count * pages_dev
    page_blocks = jnp.take(page_pool, local_ids.reshape(-1), axis=0).reshape(
        requests, NPR, 2, PAGE, HD
    )
    cache_keys, cache_values = split_pages(page_blocks, requests)
    result = attend(
        queries.reshape(requests, DRAFT, slots_per, HD),
        cache_keys,
        cache_values,
        tree_keys.reshape(requests, DRAFT, HD),
        tree_values.reshape(requests, DRAFT, HD),
        cache_len,
        position,
        reach,
    )
    mixed = result.reshape(-1, slots_per * HD)
    attended = reduce_heads(mixed, output_weight, safe_heads, head_mask, slots_per)
    new_pages = jax.vmap(refresh)(
        own_pages,
        own_len,
        own_leaf,
        own_reach,
        own_depth,
        own_keys.reshape(owned, DRAFT, HD),
        own_values.reshape(owned, DRAFT, HD),
    )
    flat_ids = own_table.reshape(-1)
    matches = (flat_ids[:, None] == jnp.arange(pages_dev, dtype=jnp.int32)[None, :]).astype(
        jnp.int32
    )
    inverse = jnp.sum(matches * jnp.arange(pages_dev, dtype=jnp.int32)[:, None], axis=0)
    cache_out = jnp.take(new_pages.reshape(pages_dev, 2, PAGE, HD), inverse, axis=0)
    return (attended, cache_out)


def solution(mesh):
    in_specs = (
        P("tok", "head"),
        P("tok", None),
        P("tok", None),
        P(None, ("head", "tok")),
        P(("tok", "head"), None, None, None),
        P("tok", None),
        P("tok", None),
        P("tok"),
        P("tok"),
    )
    out_specs = (P("tok", "head"), P(("tok", "head"), None, None, None))
    return jax.shard_map(shards, mesh=mesh, in_specs=in_specs, out_specs=out_specs, check_vma=False)
```

profile of v0, /device:TPU:2, one launch (start us, length us, event | category | flops | bytes accessed | tf_op | source)
XLA Modules:
  0.0 582.3 jit_solution(10205464197976937876)
XLA Ops:
  7.2 0.7 all-gather.9.cloned.1.call-update
  8.0 0.7 all-gather.13.cloned.1.call-update
  8.9 0.9 copy.116
  9.9 0.6 gather_fusion.1
  10.4 0.6 select_multiply_fusion.1
  11.1 0.5 all-gather.7.cloned.1.call-update
  11.7 13.6 %all-gather = bf16[8,5,2560]{2,1,0:T(8,128)(2,1)S(1)} all-gather(bf16[1,5,2560]{2,1,0:T(8,128)(2,1)} %bitcast.138), channel_id=1, replica_groups=mesh['tok'=64,'head'=8] {'head'}, dimensions={0}, use_global_device_ids=true | all-gather | bytes 230400 | tf_op jit(solution)/shard_map/all_gather | solution.py:111
  25.5 0.6 gather_fusion.2
  26.1 0.6 select_multiply_fusion
  26.8 0.5 convolution_minimum_fusion.5
  27.7 0.4 convolution_minimum_fusion.3
  28.9 0.5 fusion.58
  29.6 0.8 copy.86
  30.6 0.6 copy.75
  31.6 16.7 %all-gather.9.cloned.1.call-done = bf16[512,2560]{0,1:T(8,128)(2,1)} async-done(((bf16[512,320]{0,1:T(8,128)(2,1)}), bf16[512,2560]{0,1:T(8,128)(2,1)}) %all-gather.9.cloned.1.call-update) | async-done | bytes 2621456 | tf_op jit(solution)/shard_map/all_gather | solution.py:156
  48.3 2.5 fusion
  50.8 141.9 %all-gather.13.cloned.1.call-done = bf16[2560,512]{1,0:T(8,128)(2,1)} async-done(((bf16[40,512]{1,0:T(8,128)(2,1)}), bf16[2560,512]{1,0:T(8,128)(2,1)}) %all-gather.13.cloned.1.call-update) | async-done | bytes 2621456 | tf_op jit(solution)/shard_map/all_gather | solution.py:95
  192.7 3.3 fusion.2
  196.0 0.7 slice.107
  196.7 0.7 slice.106
  197.5 1.9 multiply_cosine_fusion
  199.4 1.1 copy.80
  200.4 0.8 copy.81
  201.2 131.7 %all-gather.11.cloned.1.call-done = bf16[2560,512]{1,0:T(8,128)(2,1)} async-done(((bf16[40,512]{1,0:T(8,128)(2,1)}), bf16[2560,512]{1,0:T(8,128)(2,1)}) %all-gather.11.cloned.1.call-update) | async-done | bytes 2621456 | tf_op jit(solution)/shard_map/all_gather | solution.py:173
  332.9 3.3 fusion.4
  337.4 0.6 fusion.59
  338.0 33.0 %all-gather.7.cloned.1.call-done = bf16[32,2,128,256]{3,2,1,0:T(8,128)(2,1)} async-done(((bf16[4,2,128,256]{3,2,1,0:T(8,128)(2,1)}), bf16[32,2,128,256]{3,2,1,0:T(8,128)(2,1)}) %all-gather.7.cloned.1.call-update) | async-done | bytes 4194320 | tf_op jit(solution)/shard_map/all_gather | solution.py:190
  371.0 5.1 gather_fusion
  376.1 2.7 copy_select_fusion
  378.8 0.5 fusion.56
  379.3 1.0 fusion.6
  380.4 0.7 fusion.7
  381.6 0.9 fusion.9
  382.5 0.5 copy.88
  383.1 131.6 %all-gather.15.cloned.1.call-done = bf16[512,2560]{0,1:T(8,128)(2,1)} async-done(((bf16[512,40]{0,1:T(8,128)(2,1)}), bf16[512,2560]{0,1:T(8,128)(2,1)}) %all-gather.15.cloned.1.call-update) | async-done | bytes 2621456 | tf_op jit(solution)/shard_map/all_gather | solution.py:119
  514.8 4.8 convolution_convert_fusion
  519.6 3.0 copy.91
  522.6 2.9 reshape.548
  525.5 4.6 copy.92
  530.1 6.2 %reshape.549 = bf16[512,2560]{0,1:T(8,128)(2,1)} reshape(bf16[512,8,64,5]{0,3,2,1:T(8,128)(2,1)} %copy.92) | data formatting | bytes 5242880 | tf_op jit(solution)/shard_map/reshape | solution.py:124
  536.4 0.6 dynamic_slice.24
  537.0 0.6 dynamic_slice.22
  539.1 0.6 gather_fusion.3
  540.6 0.5 iota_subtract_fusion
  541.3 1.0 fusion.12
  542.9 0.6 gather_fusion.4
  543.5 0.9 broadcast_select_fusion
  544.4 31.1 %reduce-scatter.2.cloned.1.call-done = bf16[512,320]{0,1:T(8,128)(2,1)} async-done(((bf16[512,2560]{0,1:T(8,128)(2,1)}), bf16[512,320]{0,1:T(8,128)(2,1)}) %reduce-scatter.2.cloned.1.call-update) | async-done | bytes 327696 | tf_op jit(solution)/shard_map/reduce_scatter | solution.py:128
  (94 shorter events, 5.6 us)
Async XLA Ops:
  7.2 19.6 %copy-start.12 = (s32[8,64]{1,0:T(8,128)S(1)}, s32[8,64]{1,0:T(8,128)}, u32[]{:S(2)}) copy-start(s32[8,64]{1,0:T(8,128)} %param.17) | copy-start | bytes 6148
  7.2 41.1 %all-gather.9.cloned.1.call-start = ((), (), s32[]{:S(2)}) async-start(), calls=%async_computation.2 | async-start | bytes 2949120 | tf_op jit(solution)/shard_map/all_gather | solution.py:156
  7.9 184.8 %all-gather.13.cloned.1.call-start = ((), (), s32[]{:S(2)}) async-start(), calls=%async_computation.4 | async-start | bytes 2662400 | tf_op jit(solution)/shard_map/all_gather | solution.py:95
  8.7 324.3 %all-gather.11.cloned.1.call-start = ((), (), s32[]{:S(2)}) async-start(), calls=%async_computation.3 | async-start | bytes 2662400 | tf_op jit(solution)/shard_map/all_gather | solution.py:173
  11.1 359.9 %all-gather.7.cloned.1.call-start = ((), (), s32[]{:S(2)}) async-start(), calls=%async_computation.1 | async-start | bytes 4718592 | tf_op jit(solution)/shard_map/all_gather | solution.py:190
  11.7 503.1 %all-gather.15.cloned.1.call-start = ((), (), s32[]{:S(2)}) async-start(), calls=%async_computation.5 | async-start | bytes 2662400 | tf_op jit(solution)/shard_map/all_gather | solution.py:119
  25.5 3.9 copy-start.9
  25.5 4.9 copy-start.8
  26.7 548.7 %reduce-scatter.2.cloned.1.call-start = ((), (), s32[]{:S(2)}) async-start(), calls=%async_computation.6 | async-start | bytes 2949120 | tf_op jit(solution)/shard_map/reduce_scatter | solution.py:128
  48.3 144.5 %copy-start = (bf16[512,2560]{0,1:T(8,128)(2,1)S(1)}, bf16[512,2560]{0,1:T(8,128)(2,1)}, u32[]{:S(2)}) copy-start(bf16[512,2560]{0,1:T(8,128)(2,1)} %all-gather.9.cloned.1.call-done) | copy-start | bytes 7864324
  50.8 145.2 %copy-start.10 = (f32[512]{0:T(512)}, f32[512]{0:T(512)S(1)}, u32[]{:S(2)}) copy-start(f32[512]{0:T(512)S(1)} %add_rsqrt_fusion) | copy-start | bytes 6148
  201.2 135.1 %copy-start.2 = (f32[512,64]{0,1:T(8,128)S(1)}, f32[512,64]{0,1:T(8,128)}, u32[]{:S(2)}) copy-start(f32[512,64]{0,1:T(8,128)} %copy.81) | copy-start | bytes 393220
  336.4 1.0 copy-start.3
  336.4 1.0 copy-start.4
  336.4 1.0 copy-start.5
  336.4 1.0 copy-start.7
  338.0 38.1 %copy-start.11 = (pred[8,4]{1,0:T(8,128)(4,1)S(1)}, pred[8,4]{1,0:T(8,128)(4,1)}, u32[]{:S(2)}) copy-start(pred[8,4]{1,0:T(8,128)(4,1)} %copy.75) | copy-start | bytes 100
  380.3 1.0 copy-start.6
  536.3 0.7 copy-start.13
  536.3 2.8 copy-start.1
Sparse Core Ops, SparseCore 0:
  10.1 38.1 all-gather.8
  51.2 141.4 all-gather.12
  195.7 137.1 all-gather.10
  334.9 36.0 all-gather.6
  373.8 140.8 all-gather.14
  536.5 38.9 reduce-scatter.1
where the time goes:
time: 583 us; the launch traced here: 582 us
  waiting for transfers between devices  488 us (84%)
  local copies, waits for them, and re-layouts  33.8 us (6%)
  matrix products  18.1 us (3%)
  between operations  16.5 us (3%)
  blocking collectives  13.6 us (2%)
  other arithmetic  12 us (2%)
    all_gather x1, waiting for transfers between devices, project_memory(): lax.all_gather(keyvalue_weight, 'tok', axis=0, tiled=True)  142 us
    all_gather x1, waiting for transfers between devices, shards(): lax.all_gather(my_query_weight, 'tok', axis=0, tiled=True)  132 us
    all_gather x1, waiting for transfers between devices, reduce_heads(): lax.all_gather(my_output_weight, 'tok', axis=1, tiled=True)  132 us
    all_gather x1, waiting for transfers between devices, shards(): page_pool = lax.all_gather(cache, 'head', axis=0, tiled=True)  33 us
    reduce_scatter x1, waiting for transfers between devices, reduce_heads(): lax.psum_scatter(partial_value.astype(jnp.float32).astype(jnp.bfloat16),...  31.1 us
    all_gather x1, waiting for transfers between devices, shards(): gathered = lax.all_gather(tokens, 'head', axis=1, tiled=True)  16.7 us
    all_gather x1, blocking collectives, reduce_heads(): blocks = lax.all_gather(output_weight, 'head', axis=1, tiled=True)  13.6 us
  transfers between devices with their start and end apart: 6, of which 6 were waited for; matrix products, arithmetic and copies ran while one was open for 7% of the time, Pallas kernels for 0%

commit v1 on v0

--- a/solution.py
+++ b/solution.py
@@ -153,7 +153,24 @@
     owned = requests // head_count
     rows_owned = owned * DRAFT
     pages_dev = cache.shape[0]
-    gathered = lax.all_gather(tokens, "head", axis=1, tiled=True)
+    ways, here, step = (lax.axis_size("head"), lax.axis_index("head"), tokens.shape[1])
+    shape = [n * ways if d == 1 else n for d, n in enumerate(tokens.shape)]
+    gathered = lax.dynamic_update_slice_in_dim(
+        jnp.zeros(shape, tokens.dtype), tokens, here * step, axis=1
+    )
+    going_up = going_down = tokens
+    for far in range(1, ways // 2 + 1):
+        going_up = lax.ppermute(going_up, "head", [(d, (d + 1) % ways) for d in range(ways)])
+        gathered = lax.dynamic_update_slice_in_dim(
+            gathered, going_up, (here - far) % ways * step, axis=1
+        )
+        if 2 * far < ways:
+            going_down = lax.ppermute(
+                going_down, "head", [(d, (d - 1) % ways) for d in range(ways)]
+            )
+            gathered = lax.dynamic_update_slice_in_dim(
+                gathered, going_down, (here + far) % ways * step, axis=1
+            )
     wide = gathered.astype(jnp.float32)
     mean_square = jnp.mean(wide * wide, axis=1, keepdims=True)
     normed = (wide * lax.rsqrt(mean_square + 1e-06)).astype(jnp.bfloat16)

time: 583 us -> 547 us (0.938)
  waiting for transfers between devices: 488 us -> 442 us
  starting transfers between devices: 0.24 us -> 9.11 us
    all_gather x1, waiting for transfers between devices: 142 us -> 98.2 us  [project_memory(): lax.all_gather(keyvalue_weight, 'tok', axis=0, tiled=True)]
    all_gather x1 -> x0, waiting for transfers between devices: 16.7 us -> none  [shards(): gathered = lax.all_gather(tokens, 'head', axis=1, tiled=True)]
    ppermute x0 -> x7, waiting for transfers between devices: none -> 15 us  [the longest x4 13.2 us: shards(): lax.ppermute(going_up, 'head', [(d, (d + 1) % ways) for d in range(ways)])]
    ppermute x0 -> x7, starting transfers between devices: none -> 8.91 us  [the longest x3 8.53 us: shards(): lax.ppermute(going_down, 'head', [(d, (d - 1) % ways) for d in range(ways)])]
  transfers between devices with their start and end apart: 6 -> 12, of which waited for: 6 -> 9; matrix products, arithmetic and copies ran while one was open for 7% -> 8% of each run, Pallas kernels for 0% -> 0%
where the time goes in v1:
time: 547 us; the launch traced here: 546 us
  waiting for transfers between devices  442 us (81%)
  local copies, waits for them, and re-layouts  36.2 us (7%)
  matrix products  18.1 us (3%)
  between operations  16.5 us (3%)
  blocking collectives  13.6 us (2%)
  other arithmetic  10.2 us (2%)
  starting transfers between devices  9.11 us (2%)
    all_gather x1, waiting for transfers between devices, shards(): lax.all_gather(my_query_weight, 'tok', axis=0, tiled=True)  132 us
    all_gather x1, waiting for transfers between devices, reduce_heads(): lax.all_gather(my_output_weight, 'tok', axis=1, tiled=True)  132 us
    all_gather x1, waiting for transfers between devices, project_memory(): lax.all_gather(keyvalue_weight, 'tok', axis=0, tiled=True)  98.2 us
    all_gather x1, waiting for transfers between devices, shards(): page_pool = lax.all_gather(cache, 'head', axis=0, tiled=True)  33.2 us
    reduce_scatter x1, waiting for transfers between devices, reduce_heads(): lax.psum_scatter(partial_value.astype(jnp.float32).astype(jnp.bfloat16),...  31 us
    all_gather x1, blocking collectives, reduce_heads(): blocks = lax.all_gather(output_weight, 'head', axis=1, tiled=True)  13.6 us
    ppermute x4, waiting for transfers between devices, shards(): lax.ppermute(going_up, 'head', [(d, (d + 1) % ways) for d in range(ways)])  13.2 us
  transfers between devices with their start and end apart: 12, of which 9 were waited for; matrix products, arithmetic and copies ran while one was open for 8% of the time, Pallas kernels for 0%

profile of v1, /device:TPU:2, one launch (start us, length us, event | category | flops | bytes accessed | tf_op | source)
XLA Modules:
  0.0 545.8 jit_solution(7027074084581715614)
XLA Ops:
  7.2 0.7 all-gather.10.cloned.1.call-update
  8.1 0.9 copy.116
  9.7 0.6 select_multiply_fusion.1
  10.4 0.7 all-gather.6.cloned.1.call-update
  11.2 2.9 collective-permute-start.1
  14.1 13.6 %all-gather = bf16[8,5,2560]{2,1,0:T(8,128)(2,1)S(1)} all-gather(bf16[1,5,2560]{2,1,0:T(8,128)(2,1)} %bitcast.138), channel_id=1, replica_groups=mesh['tok'=64,'head'=8] {'head'}, dimensions={0}, use_global_device_ids=true | all-gather | bytes 230400 | tf_op jit(solution)/shard_map/all_gather | solution.py:111
  28.4 0.6 select_multiply_fusion
  32.2 0.7 copy.75
  33.0 0.8 copy.86
  34.7 2.6 collective-permute-start.3
  37.3 4.7 collective-permute-done.2
  42.0 1.0 constant_dynamic-update-slice_fusion.6
  43.0 1.0 constant_dynamic-update-slice_fusion.5
  44.0 3.0 collective-permute-start.5
  47.0 2.7 collective-permute-done.4
  49.7 1.8 collective-permute-done.5
  51.6 5.8 %collective-permute-done.6 = bf16[512,320]{0,1:T(8,128)(2,1)S(1)} collective-permute-done((bf16[512,320]{0,1:T(8,128)(2,1)S(1)}, bf16[512,320]{0,1:T(8,128)(2,1)S(1)}, u32[]{:S(2)}, u32[]{:S(2)}) %collective-permute-start.6) | collective-permute-done | bytes 327712 | tf_op jit(solution)/shard_map/ppermute | solution.py:163
  57.4 0.6 fusion
  58.1 98.2 %all-gather.10.cloned.1.call-done = bf16[2560,512]{1,0:T(8,128)(2,1)} async-done(((bf16[40,512]{1,0:T(8,128)(2,1)}), bf16[2560,512]{1,0:T(8,128)(2,1)}) %all-gather.10.cloned.1.call-update) | async-done | bytes 2621456 | tf_op jit(solution)/shard_map/all_gather | solution.py:95
  156.3 3.3 fusion.2
  159.6 0.7 slice.107
  160.3 0.7 slice.106
  161.0 1.9 multiply_cosine_fusion
  162.9 1.1 copy.80
  164.0 0.8 copy.81
  164.7 131.7 %all-gather.8.cloned.1.call-done = bf16[2560,512]{1,0:T(8,128)(2,1)} async-done(((bf16[40,512]{1,0:T(8,128)(2,1)}), bf16[2560,512]{1,0:T(8,128)(2,1)}) %all-gather.8.cloned.1.call-update) | async-done | bytes 2621456 | tf_op jit(solution)/shard_map/all_gather | solution.py:190
  296.5 3.3 fusion.4
  301.0 0.6 fusion.61
  301.6 33.2 %all-gather.6.cloned.1.call-done = bf16[32,2,128,256]{3,2,1,0:T(8,128)(2,1)} async-done(((bf16[4,2,128,256]{3,2,1,0:T(8,128)(2,1)}), bf16[32,2,128,256]{3,2,1,0:T(8,128)(2,1)}) %all-gather.6.cloned.1.call-update) | async-done | bytes 4194320 | tf_op jit(solution)/shard_map/all_gather | solution.py:207
  334.7 5.1 gather_fusion
  339.8 2.7 copy_select_fusion
  343.0 1.0 fusion.6
  344.1 0.7 fusion.7
  345.3 0.9 fusion.9
  346.8 131.6 %all-gather.12.cloned.1.call-done = bf16[512,2560]{0,1:T(8,128)(2,1)} async-done(((bf16[512,40]{0,1:T(8,128)(2,1)}), bf16[512,2560]{0,1:T(8,128)(2,1)}) %all-gather.12.cloned.1.call-update) | async-done | bytes 2621456 | tf_op jit(solution)/shard_map/all_gather | solution.py:119
  478.5 4.8 convolution_convert_fusion
  483.3 3.0 copy.91
  486.3 2.9 reshape.548
  489.2 4.7 copy.92
  493.8 6.2 %reshape.549 = bf16[512,2560]{0,1:T(8,128)(2,1)} reshape(bf16[512,8,64,5]{0,3,2,1:T(8,128)(2,1)} %copy.92) | data formatting | bytes 5242880 | tf_op jit(solution)/shard_map/reshape | solution.py:124
  500.1 0.6 dynamic_slice.24
  500.7 0.6 dynamic_slice.22
  502.9 0.6 gather_fusion.3
  504.4 0.6 iota_subtract_fusion
  505.1 1.0 fusion.12
  506.8 0.6 gather_fusion.4
  507.4 0.9 broadcast_select_fusion
  508.3 31.0 %reduce-scatter.2.cloned.1.call-done = bf16[512,320]{0,1:T(8,128)(2,1)} async-done(((bf16[512,2560]{0,1:T(8,128)(2,1)}), bf16[512,320]{0,1:T(8,128)(2,1)}) %reduce-scatter.2.cloned.1.call-update) | async-done | bytes 327696 | tf_op jit(solution)/shard_map/reduce_scatter | solution.py:128
  (114 shorter events, 9.7 us)
Async XLA Ops:
  7.2 22.0 %copy-start.12 = (s32[8,64]{1,0:T(8,128)S(1)}, s32[8,64]{1,0:T(8,128)}, u32[]{:S(2)}) copy-start(s32[8,64]{1,0:T(8,128)} %param.17) | copy-start | bytes 6148
  7.2 149.1 %all-gather.10.cloned.1.call-start = ((), (), s32[]{:S(2)}) async-start(), calls=%async_computation.3 | async-start | bytes 2662400 | tf_op jit(solution)/shard_map/all_gather | solution.py:95
  7.9 288.6 %all-gather.8.cloned.1.call-start = ((), (), s32[]{:S(2)}) async-start(), calls=%async_computation.2 | async-start | bytes 2662400 | tf_op jit(solution)/shard_map/all_gather | solution.py:190
  10.3 324.4 %all-gather.6.cloned.1.call-start = ((), (), s32[]{:S(2)}) async-start(), calls=%async_computation.1 | async-start | bytes 4718592 | tf_op jit(solution)/shard_map/all_gather | solution.py:207
  11.1 467.4 %all-gather.12.cloned.1.call-start = ((), (), s32[]{:S(2)}) async-start(), calls=%async_computation.4 | async-start | bytes 2662400 | tf_op jit(solution)/shard_map/all_gather | solution.py:119
  11.1 22.9 %collective-permute-start = (bf16[512,320]{0,1:T(8,128)(2,1)}, bf16[512,320]{0,1:T(8,128)(2,1)}, u32[]{:S(2)}, u32[]{:S(2)}) collective-permute-start(bf16[512,320]{0,1:T(8,128)(2,1)} %param.11), channel_id=1, source_target_pairs={{0,1},{1,2},{2,3},{3,4},{4,5},{5,6},{6,7},{7,0},{8,9},{9,10},{10,1... | collective-permute-start | bytes 983048 | tf_op jit(solution)/shard_map/ppermute | solution.py:163
  11.2 23.5 %collective-permute-start.1 = (bf16[512,320]{0,1:T(8,128)(2,1)}, bf16[512,320]{0,1:T(8,128)(2,1)}, u32[]{:S(2)}, u32[]{:S(2)}) collective-permute-start(bf16[512,320]{0,1:T(8,128)(2,1)} %param.11), channel_id=1, source_target_pairs={{0,7},{1,0},{2,1},{3,2},{4,3},{5,4},{6,5},{7,6},{8,15},{9,8},{10,9... | collective-permute-start | bytes 983048 | tf_op jit(solution)/shard_map/ppermute | solution.py:168
  27.7 4.1 copy-start.9
  27.8 4.3 copy-start.8
  29.0 510.2 %reduce-scatter.2.cloned.1.call-start = ((), (), s32[]{:S(2)}) async-start(), calls=%async_computation.5 | async-start | bytes 2949120 | tf_op jit(solution)/shard_map/reduce_scatter | solution.py:128
  30.5 3.4 copy-start.6
  34.0 7.9 %collective-permute-start.2 = (bf16[512,320]{0,1:T(8,128)(2,1)}, bf16[512,320]{0,1:T(8,128)(2,1)S(1)}, u32[]{:S(2)}, u32[]{:S(2)}) collective-permute-start(bf16[512,320]{0,1:T(8,128)(2,1)} %collective-permute-done), channel_id=1, source_target_pairs={{0,1},{1,2},{2,3},{3,4},{4,5},{5,6},{6,7},{7,0},{8,9},{9,10},{10,1... | collective-permute-start | bytes 983048 | tf_op jit(solution)/shard_map/ppermute | solution.py:163
  34.7 9.3 %collective-permute-start.3 = (bf16[512,320]{0,1:T(8,128)(2,1)}, bf16[512,320]{0,1:T(8,128)(2,1)S(1)}, u32[]{:S(2)}, u32[]{:S(2)}) collective-permute-start(bf16[512,320]{0,1:T(8,128)(2,1)} %collective-permute-done.1), channel_id=1, source_target_pairs={{0,7},{1,0},{2,1},{3,2},{4,3},{5,4},{6,5},{7,6},{8,15},{9,8},{10,9... | collective-permute-start | bytes 983048 | tf_op jit(solution)/shard_map/ppermute | solution.py:168
  42.0 7.7 %collective-permute-start.4 = (bf16[512,320]{0,1:T(8,128)(2,1)S(1)}, bf16[512,320]{0,1:T(8,128)(2,1)S(1)}, u32[]{:S(2)}, u32[]{:S(2)}) collective-permute-start(bf16[512,320]{0,1:T(8,128)(2,1)S(1)} %collective-permute-done.2), channel_id=1, source_target_pairs={{0,1},{1,2},{2,3},{3,4},{4,5},{5,6},{6,7},{7,0},{8,9},{9,10},{10,1... | collective-permute-start | bytes 983048 | tf_op jit(solution)/shard_map/ppermute | solution.py:163
  44.0 7.6 %collective-permute-start.5 = (bf16[512,320]{0,1:T(8,128)(2,1)S(1)}, bf16[512,320]{0,1:T(8,128)(2,1)S(1)}, u32[]{:S(2)}, u32[]{:S(2)}) collective-permute-start(bf16[512,320]{0,1:T(8,128)(2,1)S(1)} %collective-permute-done.3), channel_id=1, source_target_pairs={{0,7},{1,0},{2,1},{3,2},{4,3},{5,4},{6,5},{7,6},{8,15},{9,8},{10,9... | collective-permute-start | bytes 983048 | tf_op jit(solution)/shard_map/ppermute | solution.py:168
  49.7 7.7 %collective-permute-start.6 = (bf16[512,320]{0,1:T(8,128)(2,1)S(1)}, bf16[512,320]{0,1:T(8,128)(2,1)S(1)}, u32[]{:S(2)}, u32[]{:S(2)}) collective-permute-start(bf16[512,320]{0,1:T(8,128)(2,1)S(1)} %collective-permute-done.4), channel_id=1, source_target_pairs={{0,1},{1,2},{2,3},{3,4},{4,5},{5,6},{6,7},{7,0},{8,9},{9,10},{10,1... | collective-permute-start | bytes 983048 | tf_op jit(solution)/shard_map/ppermute | solution.py:163
  58.0 101.5 %copy-start.10 = (f32[512]{0:T(512)}, f32[512]{0:T(512)S(1)}, u32[]{:S(2)}) copy-start(f32[512]{0:T(512)S(1)} %add_rsqrt_fusion) | copy-start | bytes 6148
  164.7 135.1 %copy-start.1 = (f32[512,64]{0,1:T(8,128)S(1)}, f32[512,64]{0,1:T(8,128)}, u32[]{:S(2)}) copy-start(f32[512,64]{0,1:T(8,128)} %copy.81) | copy-start | bytes 393220
  299.9 1.0 copy-start.2
  299.9 1.0 copy-start.3
  300.0 1.0 copy-start.4
  300.0 1.0 copy-start.7
  301.6 38.3 %copy-start.11 = (pred[8,4]{1,0:T(8,128)(4,1)S(1)}, pred[8,4]{1,0:T(8,128)(4,1)}, u32[]{:S(2)}) copy-start(pred[8,4]{1,0:T(8,128)(4,1)} %copy.75) | copy-start | bytes 100
  344.0 1.0 copy-start.5
  500.0 0.7 copy-start.13
  500.0 2.9 copy-start
Sparse Core Ops, SparseCore 0:
  10.9 145.3 all-gather.9
  159.2 137.1 all-gather.7
  298.6 36.0 all-gather.5
  337.5 140.8 all-gather.11
  500.2 38.9 reduce-scatter.1
